TPU v7x, 32 devices: a whole 2x2x4 slice. The times are simulated.
32 devices in a mesh: gx: 16 (over z, y, x), gy: 2 (over core).
Axes of the slice: x: 2, y: 2, z: 4, core: 2. Of those that a mesh axis runs over, the one named last changes fastest.
Arguments:
- load_parts: bfloat16 [16, 2, 4, 192, 384], P('gx', 'gy'), may hold values from -6 to 6
- schur: bfloat16 [16, 2, 4, 384, 384], P('gx', 'gy'), may hold values from -4 to 4
- deluxe: bfloat16 [16, 2, 4, 384, 384], P('gx', 'gy'), may hold values from -4 to 4
- panels: bfloat16 [16, 2, 4, 384, 384], P('gx', 'gy'), may hold values from -4 to 4
- coarse_inverse: float32 [128, 128], P(('gx', 'gy')), may hold values from -1 to 1
- primal_dofs: int32 [16, 2, 4], P('gx', 'gy'), may hold values from 0 to 1535
- damage_flags: int32 [16, 2, 4], P('gx', 'gy'), may hold values 0 or 1
Outputs:
- increment: bfloat16 [16, 2, 4, 192, 384], P('gx', 'gy')
Inputs may be any that keep to these rules, and one draw needn't show every extreme that they name: `primal_dofs`: each entry names a face times 384 plus a position on that face.
All inputs are finite; a program needn't handle non-finite values. No bound on the sum of `damage_flags` on one device may be relied on, other than what follows from the above.
Results may differ from a plain program's by a relative error of at most 0.003.
The roundings to bfloat16 on the way count: a program that leaves them out, or rounds other values in their place, can miss the bound.
Values may be sent and summed in bfloat16 or wider, within the bound.
No kernel may reach another device: no remote copies, remote signals or barrier semaphores. Data moves between devices by JAX's collectives and lax.ppermute only.
A program may use at most 64 MiB of HBM per device.

v0:
```python
import jax
import jax.numpy as jnp
from jax import lax
from jax.sharding import PartitionSpec as P


def with_halo(block, sides, width):
    for axis, dim in sides:
        count = lax.axis_size(axis)
        forward = [(i, i + 1) for i in range(count - 1)]
        backward = [(target, source) for source, target in forward]
        low = lax.ppermute(
            lax.slice_in_dim(block, block.shape[dim] - width, None, axis=dim), axis, forward
        )
        high = lax.ppermute(lax.slice_in_dim(block, 0, width, axis=dim), axis, backward)
        block = jnp.concatenate([low, block, high], axis=dim)
    return block


def face_mul(vectors, matrices):
    return jnp.einsum("fry,fyx->frx", vectors, matrices, preferred_element_type=jnp.float32)


def face_mul_turned(vectors, matrices):
    return jnp.einsum("fry,fxy->frx", vectors, matrices, preferred_element_type=jnp.float32)


def face_pairs(values):
    along_first = with_halo(values[0:2], (("gx", 0),), 1)
    along_second = with_halo(values[2:4], (("gy", 0),), 1)
    return jnp.stack([along_first[0], along_first[3], along_second[0], along_second[3]], axis=0)


def image_pairs(values):
    along_first = with_halo(values[0:2], (("gx", 0),), 1)
    along_second = with_halo(values[2:4], (("gy", 0),), 1)
    return jnp.stack([along_first[0], along_first[3], along_second[0], along_second[3]], axis=0)


def per_device(load_parts, schur, deluxe, panels, coarse_inverse, primal_dofs, damage_flags):
    loads_here = load_parts[0, 0]
    schur_panel = schur[0, 0]
    deluxe_panel = deluxe[0, 0]
    inverse_panel = panels[0, 0]
    primal_slots = primal_dofs[0, 0]
    flag_values = damage_flags[0, 0]
    width = loads_here.shape[2]
    primal_count = primal_slots.shape[0]
    positions = jnp.arange(4 * width, dtype=jnp.int32)
    picks = (primal_slots[:, None] == positions[None, :]).reshape(primal_count, 4, width)
    picks_half = picks.astype(jnp.bfloat16)
    picks_full = picks.astype(jnp.float32)
    flags_full = flag_values.astype(jnp.float32)

    def add_coarse(piece):
        return jnp.dot(coarse_inverse, piece.astype(jnp.float32), precision=lax.Precision.HIGHEST)

    def precondition(resid):
        scaled = face_mul_turned(resid.astype(jnp.bfloat16), deluxe_panel).astype(jnp.bfloat16)
        local_part = face_mul(scaled, inverse_panel)
        extra = face_mul(local_part.astype(jnp.bfloat16), inverse_panel)
        softened = local_part + 0.5 * flags_full[:, None, None] * extra
        primal = jnp.einsum(
            "kfx,frx->kr", picks_half, scaled, preferred_element_type=jnp.float32
        ).astype(jnp.bfloat16)
        coarse = add_coarse(lax.all_gather(primal, ("gx", "gy"), axis=0, tiled=True))
        placed = jnp.einsum("kfx,kr->frx", picks_full, coarse, precision=lax.Precision.HIGHEST)
        weighted = (softened + placed).astype(jnp.bfloat16)
        spread = face_mul(weighted, deluxe_panel).astype(jnp.bfloat16)
        return spread.astype(jnp.float32) + face_pairs(spread).astype(jnp.float32)

    def apply_operator(field):
        bent = face_mul(field.astype(jnp.bfloat16), schur_panel).astype(jnp.bfloat16)
        return bent.astype(jnp.float32) + image_pairs(bent).astype(jnp.float32)

    resid0 = loads_here.astype(jnp.float32) + face_pairs(loads_here).astype(jnp.float32)
    first = precondition(resid0)
    resid1 = resid0 - apply_operator(first)
    second = precondition(resid1)
    top = lax.psum(jnp.sum(resid1 * second, axis=(0, 2)), ("gx", "gy"))
    curved = apply_operator(second)
    bottom = lax.psum(jnp.sum(second * curved, axis=(0, 2)), ("gx", "gy"))
    step_len = top / bottom
    result = (first + step_len[:, None] * second).astype(jnp.bfloat16)
    return result[None, None]


def solution(mesh):
    return jax.shard_map(
        per_device,
        mesh=mesh,
        in_specs=(
            P("gx", "gy", None, None, None),
            P("gx", "gy", None, None, None),
            P("gx", "gy", None, None, None),
            P("gx", "gy", None, None, None),
            P(("gx", "gy"), None),
            P("gx", "gy", None),
            P("gx", "gy", None),
        ),
        out_specs=P("gx", "gy", None, None, None),
        check_vma=False,
    )
```

profile of v0, /device:TPU:10, one launch (start us, length us, event | category | flops | bytes accessed | tf_op | source)
XLA Modules:
  0.0 210.2 jit_solution(9755467577524988544)
XLA Ops:
  0.0 1.3 slice_bitcast_fusion.3
  1.3 3.4 %collective-permute-start = (bf16[1,192,384]{2,1,0:T(8,128)(2,1)S(1)}, bf16[1,192,384]{2,1,0:T(8,128)(2,1)S(1)}, u32[]{:S(2)}, u32[]{:S(2)}) collective-permute-start(bf16[1,192,384]{2,1,0:T(8,128)(2,1)S(1)} %get-tuple-element.23), channel_id=1, source_target_pairs={{0,2},{2,4},{4,6},{6,8},{8,10},{10,12},{12,14},{14,16},{16,18},{18... | collective-permute-start | bytes 442376 | tf_op jit(solution)/shard_map/ppermute | solution.py:12
  4.7 2.4 %collective-permute-start.1 = (bf16[1,192,384]{2,1,0:T(8,128)(2,1)S(1)}, bf16[1,192,384]{2,1,0:T(8,128)(2,1)S(1)}, u32[]{:S(2)}, u32[]{:S(2)}) collective-permute-start(bf16[1,192,384]{2,1,0:T(8,128)(2,1)S(1)} %get-tuple-element.24), channel_id=1, source_target_pairs={{2,0},{4,2},{6,4},{8,6},{10,8},{12,10},{14,12},{16,14},{18,16},{20... | collective-permute-start | bytes 442376 | tf_op jit(solution)/shard_map/ppermute | solution.py:15
  7.2 1.3 collective-permute-start.3
  8.5 3.0 %collective-permute-start.2 = (bf16[1,192,384]{2,1,0:T(8,128)(2,1)S(1)}, bf16[1,192,384]{2,1,0:T(8,128)(2,1)S(1)}, u32[]{:S(2)}, u32[]{:S(2)}) collective-permute-start(bf16[1,192,384]{2,1,0:T(8,128)(2,1)S(1)} %get-tuple-element.26), channel_id=1, source_target_pairs={{0,1},{2,3},{4,5},{6,7},{8,9},{10,11},{12,13},{14,15},{16,17},{18,... | collective-permute-start | bytes 442376 | tf_op jit(solution)/shard_map/ppermute | solution.py:12
  11.6 0.6 multiply_bitcast_fusion
  12.1 0.0 collective-permute-done
  12.2 0.8 collective-permute-done.1
  12.9 0.0 collective-permute-done.3
  12.9 0.0 collective-permute-done.2
  13.0 0.0 copy-start.1
  13.0 0.6 convolution_convert_fusion.5
  13.6 0.0 copy-done.17
  13.7 0.0 copy-done.20
  13.7 0.3 fusion.25
  14.0 34.1 %all-gather = bf16[32,4,192]{2,1,0:T(4,128)(2,1)} all-gather(bf16[1,4,192]{2,1,0:T(4,128)(2,1)S(1)} %fusion.25), channel_id=1, replica_groups=mesh['gx'=16,'gy'=2] {'gx','gy'}, dimensions={0}, use_global_device_ids=true | all-gather | bytes 50688 | tf_op jit(solution)/shard_map/all_gather | solution.py:66
  48.0 1.5 reshape.37
  49.6 1.5 fusion.14
  51.1 0.1 convolution_bitcast_fusion.5
  51.2 1.8 convolution_bitcast_fusion.1
  53.0 2.9 %convolution_convert_fusion.4 = bf16[4,192,384]{2,1,0:T(8,128)(2,1)S(1)} fusion(f32[4,192,384]{2,1,0:T(8,128)} %convolution_bitcast_fusion.1, f32[4,192,384]{2,1,0:T(8,128)} %fusion.14, bf16[1,1,4,384,384]{4,3,2,1,0:T(8,128)(2,1)S(1)} %copy-done.1, bf16[1,1,4,384,384]{4,3,2,1,0:T(8,128)(2,1)S(1)} %copy-done, f32[4]{0:T(128)} %multiply_bitcast_fusion), kind=kOutput, calls=%fused_computation.14 | convolution fusion | flops 454754304 | bytes 5308432 | tf_op jit(solution)/shard_map/fry,fyx->frx/dot_general | solution.py:21
  55.9 0.0 copy-start.41
  55.9 0.1 fusion.56
  56.0 3.5 %collective-permute-start.4 = (bf16[1,192,384]{2,1,0:T(8,128)(2,1)S(1)}, bf16[1,192,384]{2,1,0:T(8,128)(2,1)S(1)}, u32[]{:S(2)}, u32[]{:S(2)}) collective-permute-start(bf16[1,192,384]{2,1,0:T(8,128)(2,1)S(1)} %get-tuple-element.19), channel_id=1, source_target_pairs={{0,2},{2,4},{4,6},{6,8},{8,10},{10,12},{12,14},{14,16},{16,18},{18... | collective-permute-start | bytes 442376 | tf_op jit(solution)/shard_map/ppermute | solution.py:12
  59.5 1.3 collective-permute-start.7
  60.8 3.0 %collective-permute-start.6 = (bf16[1,192,384]{2,1,0:T(8,128)(2,1)S(1)}, bf16[1,192,384]{2,1,0:T(8,128)(2,1)S(1)}, u32[]{:S(2)}, u32[]{:S(2)}) collective-permute-start(bf16[1,192,384]{2,1,0:T(8,128)(2,1)S(1)} %get-tuple-element.21), channel_id=1, source_target_pairs={{0,1},{2,3},{4,5},{6,7},{8,9},{10,11},{12,13},{14,15},{16,17},{18,... | collective-permute-start | bytes 442376 | tf_op jit(solution)/shard_map/ppermute | solution.py:12
  63.9 4.6 %collective-permute-start.5 = (bf16[1,192,384]{2,1,0:T(8,128)(2,1)S(1)}, bf16[1,192,384]{2,1,0:T(8,128)(2,1)S(1)}, u32[]{:S(2)}, u32[]{:S(2)}) collective-permute-start(bf16[1,192,384]{2,1,0:T(8,128)(2,1)S(1)} %get-tuple-element.22), channel_id=1, source_target_pairs={{2,0},{4,2},{6,4},{8,6},{10,8},{12,10},{14,12},{16,14},{18,16},{20... | collective-permute-start | bytes 442376 | tf_op jit(solution)/shard_map/ppermute | solution.py:15
  68.5 0.0 collective-permute-done.4
  68.6 3.3 %collective-permute-done.5 = bf16[1,192,384]{2,1,0:T(8,128)(2,1)S(1)} collective-permute-done((bf16[1,192,384]{2,1,0:T(8,128)(2,1)S(1)}, bf16[1,192,384]{2,1,0:T(8,128)(2,1)S(1)}, u32[]{:S(2)}, u32[]{:S(2)}) %collective-permute-start.5) | collective-permute-done | bytes 147488 | tf_op jit(solution)/shard_map/ppermute | solution.py:15
  71.8 0.5 convolution_convert_fusion.3
  72.4 0.1 copy-done.29
  72.5 0.1 fusion.55
  72.6 3.5 %collective-permute-start.8 = (bf16[1,192,384]{2,1,0:T(8,128)(2,1)S(1)}, bf16[1,192,384]{2,1,0:T(8,128)(2,1)S(1)}, u32[]{:S(2)}, u32[]{:S(2)}) collective-permute-start(bf16[1,192,384]{2,1,0:T(8,128)(2,1)S(1)} %get-tuple-element.15), channel_id=1, source_target_pairs={{0,2},{2,4},{4,6},{6,8},{8,10},{10,12},{12,14},{14,16},{16,18},{18... | collective-permute-start | bytes 442376 | tf_op jit(solution)/shard_map/ppermute | solution.py:12
  76.1 1.3 collective-permute-start.11
  77.4 3.0 %collective-permute-start.10 = (bf16[1,192,384]{2,1,0:T(8,128)(2,1)S(1)}, bf16[1,192,384]{2,1,0:T(8,128)(2,1)S(1)}, u32[]{:S(2)}, u32[]{:S(2)}) collective-permute-start(bf16[1,192,384]{2,1,0:T(8,128)(2,1)S(1)} %get-tuple-element.17), channel_id=1, source_target_pairs={{0,1},{2,3},{4,5},{6,7},{8,9},{10,11},{12,13},{14,15},{16,17},{18,... | collective-permute-start | bytes 442376 | tf_op jit(solution)/shard_map/ppermute | solution.py:12
  80.4 3.6 %collective-permute-start.9 = (bf16[1,192,384]{2,1,0:T(8,128)(2,1)S(1)}, bf16[1,192,384]{2,1,0:T(8,128)(2,1)S(1)}, u32[]{:S(2)}, u32[]{:S(2)}) collective-permute-start(bf16[1,192,384]{2,1,0:T(8,128)(2,1)S(1)} %get-tuple-element.18), channel_id=1, source_target_pairs={{2,0},{4,2},{6,4},{8,6},{10,8},{12,10},{14,12},{16,14},{18,16},{20... | collective-permute-start | bytes 442376 | tf_op jit(solution)/shard_map/ppermute | solution.py:15
  84.1 5.0 %collective-permute-done.9 = bf16[1,192,384]{2,1,0:T(8,128)(2,1)S(1)} collective-permute-done((bf16[1,192,384]{2,1,0:T(8,128)(2,1)S(1)}, bf16[1,192,384]{2,1,0:T(8,128)(2,1)S(1)}, u32[]{:S(2)}, u32[]{:S(2)}) %collective-permute-start.9) | collective-permute-done | bytes 147488 | tf_op jit(solution)/shard_map/ppermute | solution.py:15
  89.2 0.7 convolution_convert_fusion.2
  89.9 0.3 fusion.24
  90.2 1.6 fusion.10
  91.7 35.3 %all-gather.1 = bf16[32,4,192]{2,1,0:T(4,128)(2,1)S(1)} all-gather(bf16[1,4,192]{2,1,0:T(4,128)(2,1)S(1)} %fusion.24), channel_id=1, replica_groups=mesh['gx'=16,'gy'=2] {'gx','gy'}, dimensions={0}, use_global_device_ids=true | all-gather | bytes 50688 | tf_op jit(solution)/shard_map/all_gather | solution.py:66
  127.1 0.1 convolution_bitcast_fusion.4
  127.2 1.8 convolution_bitcast_fusion
  129.0 2.9 %convolution_convert_fusion.1 = bf16[4,192,384]{2,1,0:T(8,128)(2,1)S(1)} fusion(f32[4,192,384]{2,1,0:T(8,128)} %convolution_bitcast_fusion, f32[4,192,384]{2,1,0:T(8,128)} %fusion.10, bf16[1,1,4,384,384]{4,3,2,1,0:T(8,128)(2,1)S(1)} %copy-done.1, bf16[1,1,4,384,384]{4,3,2,1,0:T(8,128)(2,1)S(1)} %copy-done, f32[4]{0:T(128)} %multiply_bitcast_fusion), kind=kOutput, calls=%fused_computation.11 | convolution fusion | flops 454754304 | bytes 5308432 | tf_op jit(solution)/shard_map/fry,fyx->frx/dot_general | solution.py:21
  131.9 0.0 copy-start.42
  131.9 0.1 fusion.54
  132.0 2.1 collective-permute-start.12
  134.1 1.3 collective-permute-start.15
  135.4 3.0 %collective-permute-start.14 = (bf16[1,192,384]{2,1,0:T(8,128)(2,1)S(1)}, bf16[1,192,384]{2,1,0:T(8,128)(2,1)S(1)}, u32[]{:S(2)}, u32[]{:S(2)}) collective-permute-start(bf16[1,192,384]{2,1,0:T(8,128)(2,1)S(1)} %get-tuple-element.13), channel_id=1, source_target_pairs={{0,1},{2,3},{4,5},{6,7},{8,9},{10,11},{12,13},{14,15},{16,17},{18,... | collective-permute-start | bytes 442376 | tf_op jit(solution)/shard_map/ppermute | solution.py:12
  138.4 3.9 %collective-permute-start.13 = (bf16[1,192,384]{2,1,0:T(8,128)(2,1)S(1)}, bf16[1,192,384]{2,1,0:T(8,128)(2,1)S(1)}, u32[]{:S(2)}, u32[]{:S(2)}) collective-permute-start(bf16[1,192,384]{2,1,0:T(8,128)(2,1)S(1)} %get-tuple-element.14), channel_id=1, source_target_pairs={{2,0},{4,2},{6,4},{8,6},{10,8},{12,10},{14,12},{16,14},{18,16},{20... | collective-permute-start | bytes 442376 | tf_op jit(solution)/shard_map/ppermute | solution.py:15
  142.4 3.9 %collective-permute-done.13 = bf16[1,192,384]{2,1,0:T(8,128)(2,1)S(1)} collective-permute-done((bf16[1,192,384]{2,1,0:T(8,128)(2,1)S(1)}, bf16[1,192,384]{2,1,0:T(8,128)(2,1)S(1)}, u32[]{:S(2)}, u32[]{:S(2)}) %collective-permute-start.13) | collective-permute-done | bytes 147488 | tf_op jit(solution)/shard_map/ppermute | solution.py:15
  146.4 0.5 convolution_convert_fusion
  147.0 0.0 copy-start.3
  147.0 0.0 copy-start.5
  147.0 0.1 fusion.53
  147.1 2.9 %collective-permute-start.16 = (bf16[1,192,384]{2,1,0:T(8,128)(2,1)S(1)}, bf16[1,192,384]{2,1,0:T(8,128)(2,1)S(1)}, u32[]{:S(2)}, u32[]{:S(2)}) collective-permute-start(bf16[1,192,384]{2,1,0:T(8,128)(2,1)S(1)} %get-tuple-element.7), channel_id=1, source_target_pairs={{0,2},{2,4},{4,6},{6,8},{8,10},{10,12},{12,14},{14,16},{16,18},{18... | collective-permute-start | bytes 442376 | tf_op jit(solution)/shard_map/ppermute | solution.py:12
  149.9 1.3 collective-permute-start.19
  151.2 3.0 %collective-permute-start.18 = (bf16[1,192,384]{2,1,0:T(8,128)(2,1)S(1)}, bf16[1,192,384]{2,1,0:T(8,128)(2,1)S(1)}, u32[]{:S(2)}, u32[]{:S(2)}) collective-permute-start(bf16[1,192,384]{2,1,0:T(8,128)(2,1)S(1)} %get-tuple-element.9), channel_id=1, source_target_pairs={{0,1},{2,3},{4,5},{6,7},{8,9},{10,11},{12,13},{14,15},{16,17},{18,... | collective-permute-start | bytes 442376 | tf_op jit(solution)/shard_map/ppermute | solution.py:12
  154.3 3.4 %collective-permute-start.17 = (bf16[1,192,384]{2,1,0:T(8,128)(2,1)S(1)}, bf16[1,192,384]{2,1,0:T(8,128)(2,1)S(1)}, u32[]{:S(2)}, u32[]{:S(2)}) collective-permute-start(bf16[1,192,384]{2,1,0:T(8,128)(2,1)S(1)} %get-tuple-element.10), channel_id=1, source_target_pairs={{2,0},{4,2},{6,4},{8,6},{10,8},{12,10},{14,12},{16,14},{18,16},{20... | collective-permute-start | bytes 442376 | tf_op jit(solution)/shard_map/ppermute | solution.py:15
  157.8 0.6 multiply_reduce_fusion.1
  158.4 3.8 %collective-permute-done.17 = bf16[1,192,384]{2,1,0:T(8,128)(2,1)S(1)} collective-permute-done((bf16[1,192,384]{2,1,0:T(8,128)(2,1)S(1)}, bf16[1,192,384]{2,1,0:T(8,128)(2,1)S(1)}, u32[]{:S(2)}, u32[]{:S(2)}) %collective-permute-start.17) | collective-permute-done | bytes 147488 | tf_op jit(solution)/shard_map/ppermute | solution.py:15
  162.2 0.4 multiply_reduce_fusion
  162.6 45.2 %all-reduce = (f32[192]{0:T(256)S(1)}, f32[192]{0:T(256)S(1)}) all-reduce(f32[192]{0:T(256)S(1)} %multiply_reduce_fusion.1, f32[192]{0:T(256)S(1)} %multiply_reduce_fusion), channel_id=1, replica_groups=mesh['gx'=16,'gy'=2] {'gx','gy'}, use_global_device_ids=true, to_apply=%region_1.0 | all-reduce | flops 384 | bytes 3072 | tf_op jit(solution)/shard_map/psum | solution.py:80
  207.9 2.3 %fusion.30 = bf16[1,1,4,192,384]{4,3,2,1,0:T(8,128)(2,1)} fusion(bf16[4,192,384]{2,1,0:T(8,128)(2,1)S(1)} %convolution_convert_fusion.1, bf16[4,192,384]{2,1,0:T(8,128)(2,1)S(1)} %convolution_convert_fusion.4, f32[192]{0:T(256)S(1)} %div.3, bf16[1,192,384]{2,1,0:T(8,128)(2,1)S(1)} %copy-done.26, bf16[1,192,384]{2,1,0:T(8,128)(2,1)S(1)} %copy-done.28, ...), kind=kLoop, calls=%fused_computation.46 | loop fusion | flops 4423680 | bytes 2949888 | tf_op jit(solution)/shard_map/broadcast_in_dim | solution.py:85
  (94 shorter events, 0.2 us)
Async XLA Ops:
  0.0 12.9 %copy-start = (bf16[1,1,4,384,384]{4,3,2,1,0:T(8,128)(2,1)S(1)}, bf16[1,1,4,384,384]{4,3,2,1,0:T(8,128)(2,1)}, u32[]{:S(2)}) copy-start(bf16[1,1,4,384,384]{4,3,2,1,0:T(8,128)(2,1)} %param.9) | copy-start | bytes 3538948
  0.0 13.0 %copy-start.2 = (bf16[1,1,4,192,384]{4,3,2,1,0:T(8,128)(2,1)S(1)}, bf16[1,1,4,192,384]{4,3,2,1,0:T(8,128)(2,1)}, u32[]{:S(2)}) copy-start(bf16[1,1,4,192,384]{4,3,2,1,0:T(8,128)(2,1)} %param.7) | copy-start | bytes 1769476
  0.0 11.5 %copy-start.43 = (s32[1,1,4]{2,1,0:T(1,128)S(1)}, s32[1,1,4]{2,1,0:T(1,128)}, u32[]{:S(2)}) copy-start(s32[1,1,4]{2,1,0:T(1,128)} %param.13) | copy-start | bytes 52
  1.3 10.8 %collective-permute-start = (bf16[1,192,384]{2,1,0:T(8,128)(2,1)S(1)}, bf16[1,192,384]{2,1,0:T(8,128)(2,1)S(1)}, u32[]{:S(2)}, u32[]{:S(2)}) collective-permute-start(bf16[1,192,384]{2,1,0:T(8,128)(2,1)S(1)} %get-tuple-element.23), channel_id=1, source_target_pairs={{0,2},{2,4},{4,6},{6,8},{8,10},{10,12},{12,14},{14,16},{16,18},{18... | collective-permute-start | bytes 442376 | tf_op jit(solution)/shard_map/ppermute | solution.py:12
  4.7 8.2 %collective-permute-start.1 = (bf16[1,192,384]{2,1,0:T(8,128)(2,1)S(1)}, bf16[1,192,384]{2,1,0:T(8,128)(2,1)S(1)}, u32[]{:S(2)}, u32[]{:S(2)}) collective-permute-start(bf16[1,192,384]{2,1,0:T(8,128)(2,1)S(1)} %get-tuple-element.24), channel_id=1, source_target_pairs={{2,0},{4,2},{6,4},{8,6},{10,8},{12,10},{14,12},{16,14},{18,16},{20... | collective-permute-start | bytes 442376 | tf_op jit(solution)/shard_map/ppermute | solution.py:15
  7.2 5.7 %collective-permute-start.3 = (bf16[1,192,384]{2,1,0:T(8,128)(2,1)S(1)}, bf16[1,192,384]{2,1,0:T(8,128)(2,1)S(1)}, u32[]{:S(2)}, u32[]{:S(2)}) collective-permute-start(bf16[1,192,384]{2,1,0:T(8,128)(2,1)S(1)} %get-tuple-element.25), channel_id=1, source_target_pairs={{1,0},{3,2},{5,4},{7,6},{9,8},{11,10},{13,12},{15,14},{17,16},{19,... | collective-permute-start | bytes 442376 | tf_op jit(solution)/shard_map/ppermute | solution.py:15
  8.5 4.5 %collective-permute-start.2 = (bf16[1,192,384]{2,1,0:T(8,128)(2,1)S(1)}, bf16[1,192,384]{2,1,0:T(8,128)(2,1)S(1)}, u32[]{:S(2)}, u32[]{:S(2)}) collective-permute-start(bf16[1,192,384]{2,1,0:T(8,128)(2,1)S(1)} %get-tuple-element.26), channel_id=1, source_target_pairs={{0,1},{2,3},{4,5},{6,7},{8,9},{10,11},{12,13},{14,15},{16,17},{18,... | collective-permute-start | bytes 442376 | tf_op jit(solution)/shard_map/ppermute | solution.py:12
  12.1 1.6 copy-start.40
  12.1 1.5 copy-start.11
  12.9 0.7 copy-start.14
  12.9 0.7 copy-start.17
  13.0 0.7 copy-start.20
  13.0 36.6 %copy-start.1 = (bf16[1,1,4,384,384]{4,3,2,1,0:T(8,128)(2,1)S(1)}, bf16[1,1,4,384,384]{4,3,2,1,0:T(8,128)(2,1)}, u32[]{:S(2)}) copy-start(bf16[1,1,4,384,384]{4,3,2,1,0:T(8,128)(2,1)} %param.10) | copy-start | bytes 3538948
  49.6 1.6 copy-start.10
  49.6 1.6 copy-start.39
  55.9 15.9 %copy-start.41 = (bf16[1,1,4,384,384]{4,3,2,1,0:T(8,128)(2,1)S(1)}, bf16[1,1,4,384,384]{4,3,2,1,0:T(8,128)(2,1)}, u32[]{:S(2)}) copy-start(bf16[1,1,4,384,384]{4,3,2,1,0:T(8,128)(2,1)} %param.8) | copy-start | bytes 3538948
  56.0 12.5 %collective-permute-start.4 = (bf16[1,192,384]{2,1,0:T(8,128)(2,1)S(1)}, bf16[1,192,384]{2,1,0:T(8,128)(2,1)S(1)}, u32[]{:S(2)}, u32[]{:S(2)}) collective-permute-start(bf16[1,192,384]{2,1,0:T(8,128)(2,1)S(1)} %get-tuple-element.19), channel_id=1, source_target_pairs={{0,2},{2,4},{4,6},{6,8},{8,10},{10,12},{12,14},{14,16},{16,18},{18... | collective-permute-start | bytes 442376 | tf_op jit(solution)/shard_map/ppermute | solution.py:12
  59.5 9.0 %collective-permute-start.7 = (bf16[1,192,384]{2,1,0:T(8,128)(2,1)S(1)}, bf16[1,192,384]{2,1,0:T(8,128)(2,1)S(1)}, u32[]{:S(2)}, u32[]{:S(2)}) collective-permute-start(bf16[1,192,384]{2,1,0:T(8,128)(2,1)S(1)} %get-tuple-element.20), channel_id=1, source_target_pairs={{1,0},{3,2},{5,4},{7,6},{9,8},{11,10},{13,12},{15,14},{17,16},{19,... | collective-permute-start | bytes 442376 | tf_op jit(solution)/shard_map/ppermute | solution.py:15
  60.8 7.7 %collective-permute-start.6 = (bf16[1,192,384]{2,1,0:T(8,128)(2,1)S(1)}, bf16[1,192,384]{2,1,0:T(8,128)(2,1)S(1)}, u32[]{:S(2)}, u32[]{:S(2)}) collective-permute-start(bf16[1,192,384]{2,1,0:T(8,128)(2,1)S(1)} %get-tuple-element.21), channel_id=1, source_target_pairs={{0,1},{2,3},{4,5},{6,7},{8,9},{10,11},{12,13},{14,15},{16,17},{18,... | collective-permute-start | bytes 442376 | tf_op jit(solution)/shard_map/ppermute | solution.py:12
  63.9 7.9 %collective-permute-start.5 = (bf16[1,192,384]{2,1,0:T(8,128)(2,1)S(1)}, bf16[1,192,384]{2,1,0:T(8,128)(2,1)S(1)}, u32[]{:S(2)}, u32[]{:S(2)}) collective-permute-start(bf16[1,192,384]{2,1,0:T(8,128)(2,1)S(1)} %get-tuple-element.22), channel_id=1, source_target_pairs={{2,0},{4,2},{6,4},{8,6},{10,8},{12,10},{14,12},{16,14},{18,16},{20... | collective-permute-start | bytes 442376 | tf_op jit(solution)/shard_map/ppermute | solution.py:15
  68.5 3.8 %copy-start.23 = (bf16[1,192,384]{2,1,0:T(8,128)(2,1)}, bf16[1,192,384]{2,1,0:T(8,128)(2,1)S(1)}, u32[]{:S(2)}) copy-start(bf16[1,192,384]{2,1,0:T(8,128)(2,1)S(1)} %collective-permute-done.4) | copy-start | bytes 442372
  68.6 3.8 %copy-start.25 = (bf16[1,192,384]{2,1,0:T(8,128)(2,1)}, bf16[1,192,384]{2,1,0:T(8,128)(2,1)S(1)}, u32[]{:S(2)}) copy-start(bf16[1,192,384]{2,1,0:T(8,128)(2,1)S(1)} %collective-permute-done.7) | copy-start | bytes 442372
  68.6 3.8 %copy-start.27 = (bf16[1,192,384]{2,1,0:T(8,128)(2,1)}, bf16[1,192,384]{2,1,0:T(8,128)(2,1)S(1)}, u32[]{:S(2)}) copy-start(bf16[1,192,384]{2,1,0:T(8,128)(2,1)S(1)} %collective-permute-done.6) | copy-start | bytes 442372
  71.8 0.6 copy-start.29
  72.5 17.4 %copy-start.4 = (bf16[4,192,384]{2,1,0:T(8,128)(2,1)}, bf16[4,192,384]{2,1,0:T(8,128)(2,1)S(1)}, u32[]{:S(2)}) copy-start(bf16[4,192,384]{2,1,0:T(8,128)(2,1)S(1)} %convolution_convert_fusion.3) | copy-start | bytes 1769476
  72.5 16.7 %copy-start.12 = (bf16[1,192,384]{2,1,0:T(8,128)(2,1)S(1)}, bf16[1,192,384]{2,1,0:T(8,128)(2,1)}, u32[]{:S(2)}) copy-start(bf16[1,192,384]{2,1,0:T(8,128)(2,1)} %copy-done.11) | copy-start | bytes 442372
  72.5 16.7 %copy-start.15 = (bf16[1,192,384]{2,1,0:T(8,128)(2,1)S(1)}, bf16[1,192,384]{2,1,0:T(8,128)(2,1)}, u32[]{:S(2)}) copy-start(bf16[1,192,384]{2,1,0:T(8,128)(2,1)} %copy-done.14) | copy-start | bytes 442372
  72.5 16.7 %copy-start.18 = (bf16[1,192,384]{2,1,0:T(8,128)(2,1)S(1)}, bf16[1,192,384]{2,1,0:T(8,128)(2,1)}, u32[]{:S(2)}) copy-start(bf16[1,192,384]{2,1,0:T(8,128)(2,1)} %copy-done.17) | copy-start | bytes 442372
  72.5 16.7 %copy-start.21 = (bf16[1,192,384]{2,1,0:T(8,128)(2,1)S(1)}, bf16[1,192,384]{2,1,0:T(8,128)(2,1)}, u32[]{:S(2)}) copy-start(bf16[1,192,384]{2,1,0:T(8,128)(2,1)} %copy-done.20) | copy-start | bytes 442372
  72.6 11.5 %collective-permute-start.8 = (bf16[1,192,384]{2,1,0:T(8,128)(2,1)S(1)}, bf16[1,192,384]{2,1,0:T(8,128)(2,1)S(1)}, u32[]{:S(2)}, u32[]{:S(2)}) collective-permute-start(bf16[1,192,384]{2,1,0:T(8,128)(2,1)S(1)} %get-tuple-element.15), channel_id=1, source_target_pairs={{0,2},{2,4},{4,6},{6,8},{8,10},{10,12},{12,14},{14,16},{16,18},{18... | collective-permute-start | bytes 442376 | tf_op jit(solution)/shard_map/ppermute | solution.py:12
  76.1 8.0 %collective-permute-start.11 = (bf16[1,192,384]{2,1,0:T(8,128)(2,1)S(1)}, bf16[1,192,384]{2,1,0:T(8,128)(2,1)S(1)}, u32[]{:S(2)}, u32[]{:S(2)}) collective-permute-start(bf16[1,192,384]{2,1,0:T(8,128)(2,1)S(1)} %get-tuple-element.16), channel_id=1, source_target_pairs={{1,0},{3,2},{5,4},{7,6},{9,8},{11,10},{13,12},{15,14},{17,16},{19,... | collective-permute-start | bytes 442376 | tf_op jit(solution)/shard_map/ppermute | solution.py:15
  77.4 6.7 %collective-permute-start.10 = (bf16[1,192,384]{2,1,0:T(8,128)(2,1)S(1)}, bf16[1,192,384]{2,1,0:T(8,128)(2,1)S(1)}, u32[]{:S(2)}, u32[]{:S(2)}) collective-permute-start(bf16[1,192,384]{2,1,0:T(8,128)(2,1)S(1)} %get-tuple-element.17), channel_id=1, source_target_pairs={{0,1},{2,3},{4,5},{6,7},{8,9},{10,11},{12,13},{14,15},{16,17},{18,... | collective-permute-start | bytes 442376 | tf_op jit(solution)/shard_map/ppermute | solution.py:12
  80.4 8.7 %collective-permute-start.9 = (bf16[1,192,384]{2,1,0:T(8,128)(2,1)S(1)}, bf16[1,192,384]{2,1,0:T(8,128)(2,1)S(1)}, u32[]{:S(2)}, u32[]{:S(2)}) collective-permute-start(bf16[1,192,384]{2,1,0:T(8,128)(2,1)S(1)} %get-tuple-element.18), channel_id=1, source_target_pairs={{2,0},{4,2},{6,4},{8,6},{10,8},{12,10},{14,12},{16,14},{18,16},{20... | collective-permute-start | bytes 442376 | tf_op jit(solution)/shard_map/ppermute | solution.py:15
  84.1 5.8 %copy-start.31 = (bf16[1,192,384]{2,1,0:T(8,128)(2,1)}, bf16[1,192,384]{2,1,0:T(8,128)(2,1)S(1)}, u32[]{:S(2)}) copy-start(bf16[1,192,384]{2,1,0:T(8,128)(2,1)S(1)} %collective-permute-done.8) | copy-start | bytes 442372
  84.1 5.8 %copy-start.33 = (bf16[1,192,384]{2,1,0:T(8,128)(2,1)}, bf16[1,192,384]{2,1,0:T(8,128)(2,1)S(1)}, u32[]{:S(2)}) copy-start(bf16[1,192,384]{2,1,0:T(8,128)(2,1)S(1)} %collective-permute-done.11) | copy-start | bytes 442372
  84.1 5.8 %copy-start.35 = (bf16[1,192,384]{2,1,0:T(8,128)(2,1)}, bf16[1,192,384]{2,1,0:T(8,128)(2,1)S(1)}, u32[]{:S(2)}) copy-start(bf16[1,192,384]{2,1,0:T(8,128)(2,1)S(1)} %collective-permute-done.10) | copy-start | bytes 442372
  89.2 0.7 copy-start.37
  131.9 14.4 %copy-start.42 = (bf16[1,1,4,384,384]{4,3,2,1,0:T(8,128)(2,1)S(1)}, bf16[1,1,4,384,384]{4,3,2,1,0:T(8,128)(2,1)}, u32[]{:S(2)}) copy-start(bf16[1,1,4,384,384]{4,3,2,1,0:T(8,128)(2,1)} %param.8) | copy-start | bytes 3538948
  132.0 10.3 %collective-permute-start.12 = (bf16[1,192,384]{2,1,0:T(8,128)(2,1)S(1)}, bf16[1,192,384]{2,1,0:T(8,128)(2,1)S(1)}, u32[]{:S(2)}, u32[]{:S(2)}) collective-permute-start(bf16[1,192,384]{2,1,0:T(8,128)(2,1)S(1)} %get-tuple-element.11), channel_id=1, source_target_pairs={{0,2},{2,4},{4,6},{6,8},{8,10},{10,12},{12,14},{14,16},{16,18},{18... | collective-permute-start | bytes 442376 | tf_op jit(solution)/shard_map/ppermute | solution.py:12
  134.1 8.3 %collective-permute-start.15 = (bf16[1,192,384]{2,1,0:T(8,128)(2,1)S(1)}, bf16[1,192,384]{2,1,0:T(8,128)(2,1)S(1)}, u32[]{:S(2)}, u32[]{:S(2)}) collective-permute-start(bf16[1,192,384]{2,1,0:T(8,128)(2,1)S(1)} %get-tuple-element.12), channel_id=1, source_target_pairs={{1,0},{3,2},{5,4},{7,6},{9,8},{11,10},{13,12},{15,14},{17,16},{19,... | collective-permute-start | bytes 442376 | tf_op jit(solution)/shard_map/ppermute | solution.py:15
  135.4 7.0 %collective-permute-start.14 = (bf16[1,192,384]{2,1,0:T(8,128)(2,1)S(1)}, bf16[1,192,384]{2,1,0:T(8,128)(2,1)S(1)}, u32[]{:S(2)}, u32[]{:S(2)}) collective-permute-start(bf16[1,192,384]{2,1,0:T(8,128)(2,1)S(1)} %get-tuple-element.13), channel_id=1, source_target_pairs={{0,1},{2,3},{4,5},{6,7},{8,9},{10,11},{12,13},{14,15},{16,17},{18,... | collective-permute-start | bytes 442376 | tf_op jit(solution)/shard_map/ppermute | solution.py:12
  138.4 7.9 %collective-permute-start.13 = (bf16[1,192,384]{2,1,0:T(8,128)(2,1)S(1)}, bf16[1,192,384]{2,1,0:T(8,128)(2,1)S(1)}, u32[]{:S(2)}, u32[]{:S(2)}) collective-permute-start(bf16[1,192,384]{2,1,0:T(8,128)(2,1)S(1)} %get-tuple-element.14), channel_id=1, source_target_pairs={{2,0},{4,2},{6,4},{8,6},{10,8},{12,10},{14,12},{16,14},{18,16},{20... | collective-permute-start | bytes 442376 | tf_op jit(solution)/shard_map/ppermute | solution.py:15
  142.4 19.9 %copy-start.6 = (bf16[1,192,384]{2,1,0:T(8,128)(2,1)}, bf16[1,192,384]{2,1,0:T(8,128)(2,1)S(1)}, u32[]{:S(2)}) copy-start(bf16[1,192,384]{2,1,0:T(8,128)(2,1)S(1)} %collective-permute-done.12) | copy-start | bytes 442372
  142.4 19.8 %copy-start.7 = (bf16[1,192,384]{2,1,0:T(8,128)(2,1)}, bf16[1,192,384]{2,1,0:T(8,128)(2,1)S(1)}, u32[]{:S(2)}) copy-start(bf16[1,192,384]{2,1,0:T(8,128)(2,1)S(1)} %collective-permute-done.15) | copy-start | bytes 442372
  142.4 19.8 %copy-start.8 = (bf16[1,192,384]{2,1,0:T(8,128)(2,1)}, bf16[1,192,384]{2,1,0:T(8,128)(2,1)S(1)}, u32[]{:S(2)}) copy-start(bf16[1,192,384]{2,1,0:T(8,128)(2,1)S(1)} %collective-permute-done.14) | copy-start | bytes 442372
  146.4 15.9 %copy-start.9 = (bf16[1,192,384]{2,1,0:T(8,128)(2,1)}, bf16[1,192,384]{2,1,0:T(8,128)(2,1)S(1)}, u32[]{:S(2)}) copy-start(bf16[1,192,384]{2,1,0:T(8,128)(2,1)S(1)} %collective-permute-done.13) | copy-start | bytes 442372
  146.4 11.3 %copy-start.13 = (bf16[1,192,384]{2,1,0:T(8,128)(2,1)S(1)}, bf16[1,192,384]{2,1,0:T(8,128)(2,1)}, u32[]{:S(2)}) copy-start(bf16[1,192,384]{2,1,0:T(8,128)(2,1)} %copy-done.11) | copy-start | bytes 442372
  146.4 11.3 %copy-start.16 = (bf16[1,192,384]{2,1,0:T(8,128)(2,1)S(1)}, bf16[1,192,384]{2,1,0:T(8,128)(2,1)}, u32[]{:S(2)}) copy-start(bf16[1,192,384]{2,1,0:T(8,128)(2,1)} %copy-done.14) | copy-start | bytes 442372
  146.4 11.3 %copy-start.19 = (bf16[1,192,384]{2,1,0:T(8,128)(2,1)S(1)}, bf16[1,192,384]{2,1,0:T(8,128)(2,1)}, u32[]{:S(2)}) copy-start(bf16[1,192,384]{2,1,0:T(8,128)(2,1)} %copy-done.17) | copy-start | bytes 442372
  146.4 11.3 %copy-start.22 = (bf16[1,192,384]{2,1,0:T(8,128)(2,1)S(1)}, bf16[1,192,384]{2,1,0:T(8,128)(2,1)}, u32[]{:S(2)}) copy-start(bf16[1,192,384]{2,1,0:T(8,128)(2,1)} %copy-done.20) | copy-start | bytes 442372
  146.4 11.3 %copy-start.32 = (bf16[1,192,384]{2,1,0:T(8,128)(2,1)S(1)}, bf16[1,192,384]{2,1,0:T(8,128)(2,1)}, u32[]{:S(2)}) copy-start(bf16[1,192,384]{2,1,0:T(8,128)(2,1)} %copy-done.31) | copy-start | bytes 442372
  146.4 11.3 %copy-start.34 = (bf16[1,192,384]{2,1,0:T(8,128)(2,1)S(1)}, bf16[1,192,384]{2,1,0:T(8,128)(2,1)}, u32[]{:S(2)}) copy-start(bf16[1,192,384]{2,1,0:T(8,128)(2,1)} %copy-done.33) | copy-start | bytes 442372
  146.4 11.3 %copy-start.36 = (bf16[1,192,384]{2,1,0:T(8,128)(2,1)S(1)}, bf16[1,192,384]{2,1,0:T(8,128)(2,1)}, u32[]{:S(2)}) copy-start(bf16[1,192,384]{2,1,0:T(8,128)(2,1)} %copy-done.35) | copy-start | bytes 442372
  146.4 11.3 %copy-start.38 = (bf16[1,192,384]{2,1,0:T(8,128)(2,1)S(1)}, bf16[1,192,384]{2,1,0:T(8,128)(2,1)}, u32[]{:S(2)}) copy-start(bf16[1,192,384]{2,1,0:T(8,128)(2,1)} %copy-done.37) | copy-start | bytes 442372
  147.0 10.8 %copy-start.3 = (bf16[1,1,4,192,384]{4,3,2,1,0:T(8,128)(2,1)S(1)}, bf16[1,1,4,192,384]{4,3,2,1,0:T(8,128)(2,1)}, u32[]{:S(2)}) copy-start(bf16[1,1,4,192,384]{4,3,2,1,0:T(8,128)(2,1)} %param.7) | copy-start | bytes 1769476
  147.0 10.8 %copy-start.5 = (bf16[4,192,384]{2,1,0:T(8,128)(2,1)S(1)}, bf16[4,192,384]{2,1,0:T(8,128)(2,1)}, u32[]{:S(2)}) copy-start(bf16[4,192,384]{2,1,0:T(8,128)(2,1)} %copy-done.4) | copy-start | bytes 1769476
  147.1 11.3 %collective-permute-start.16 = (bf16[1,192,384]{2,1,0:T(8,128)(2,1)S(1)}, bf16[1,192,384]{2,1,0:T(8,128)(2,1)S(1)}, u32[]{:S(2)}, u32[]{:S(2)}) collective-permute-start(bf16[1,192,384]{2,1,0:T(8,128)(2,1)S(1)} %get-tuple-element.7), channel_id=1, source_target_pairs={{0,2},{2,4},{4,6},{6,8},{8,10},{10,12},{12,14},{14,16},{16,18},{18... | collective-permute-start | bytes 442376 | tf_op jit(solution)/shard_map/ppermute | solution.py:12
  149.9 8.4 %collective-permute-start.19 = (bf16[1,192,384]{2,1,0:T(8,128)(2,1)S(1)}, bf16[1,192,384]{2,1,0:T(8,128)(2,1)S(1)}, u32[]{:S(2)}, u32[]{:S(2)}) collective-permute-start(bf16[1,192,384]{2,1,0:T(8,128)(2,1)S(1)} %get-tuple-element.8), channel_id=1, source_target_pairs={{1,0},{3,2},{5,4},{7,6},{9,8},{11,10},{13,12},{15,14},{17,16},{19,... | collective-permute-start | bytes 442376 | tf_op jit(solution)/shard_map/ppermute | solution.py:15
  151.2 7.1 %collective-permute-start.18 = (bf16[1,192,384]{2,1,0:T(8,128)(2,1)S(1)}, bf16[1,192,384]{2,1,0:T(8,128)(2,1)S(1)}, u32[]{:S(2)}, u32[]{:S(2)}) collective-permute-start(bf16[1,192,384]{2,1,0:T(8,128)(2,1)S(1)} %get-tuple-element.9), channel_id=1, source_target_pairs={{0,1},{2,3},{4,5},{6,7},{8,9},{10,11},{12,13},{14,15},{16,17},{18,... | collective-permute-start | bytes 442376 | tf_op jit(solution)/shard_map/ppermute | solution.py:12
  154.3 7.9 %collective-permute-start.17 = (bf16[1,192,384]{2,1,0:T(8,128)(2,1)S(1)}, bf16[1,192,384]{2,1,0:T(8,128)(2,1)S(1)}, u32[]{:S(2)}, u32[]{:S(2)}) collective-permute-start(bf16[1,192,384]{2,1,0:T(8,128)(2,1)S(1)} %get-tuple-element.10), channel_id=1, source_target_pairs={{2,0},{4,2},{6,4},{8,6},{10,8},{12,10},{14,12},{16,14},{18,16},{20... | collective-permute-start | bytes 442376 | tf_op jit(solution)/shard_map/ppermute | solution.py:15
  158.3 49.5 %copy-start.24 = (bf16[1,192,384]{2,1,0:T(8,128)(2,1)S(1)}, bf16[1,192,384]{2,1,0:T(8,128)(2,1)}, u32[]{:S(2)}) copy-start(bf16[1,192,384]{2,1,0:T(8,128)(2,1)} %copy-done.23) | copy-start | bytes 442372
  158.3 49.5 %copy-start.26 = (bf16[1,192,384]{2,1,0:T(8,128)(2,1)S(1)}, bf16[1,192,384]{2,1,0:T(8,128)(2,1)}, u32[]{:S(2)}) copy-start(bf16[1,192,384]{2,1,0:T(8,128)(2,1)} %copy-done.25) | copy-start | bytes 442372
  158.3 49.5 %copy-start.28 = (bf16[1,192,384]{2,1,0:T(8,128)(2,1)S(1)}, bf16[1,192,384]{2,1,0:T(8,128)(2,1)}, u32[]{:S(2)}) copy-start(bf16[1,192,384]{2,1,0:T(8,128)(2,1)} %copy-done.27) | copy-start | bytes 442372
  158.4 49.5 %copy-start.30 = (bf16[1,192,384]{2,1,0:T(8,128)(2,1)S(1)}, bf16[1,192,384]{2,1,0:T(8,128)(2,1)}, u32[]{:S(2)}) copy-start(bf16[1,192,384]{2,1,0:T(8,128)(2,1)} %copy-done.29) | copy-start | bytes 442372
where the time goes:
time: 211 us; the launch traced here: 210 us
  blocking collectives  115 us (55%)
  starting transfers between devices  55 us (26%)
  waiting for transfers between devices  16.9 us (8%)
  matrix products  15.6 us (7%)
  other arithmetic  3.87 us (2%)
  local copies, waits for them, and re-layouts  3.46 us (2%)
    all_gather x2, blocking collectives, precondition(): lax.all_gather(primal, ('gx', 'gy'), axis=0, tiled=True)  69.4 us
    psum x1, blocking collectives, per_device(): top = lax.psum(jnp.sum(resid1 * second, axis=(0, 2)), ('gx', 'gy'))  45.2 us
    ppermute x10, starting transfers between devices, with_halo(): lax.ppermute(lax.slice_in_dim(block, block.shape[dim] - width, None, axis...  30.5 us
    ppermute x10, starting transfers between devices, with_halo(): lax.ppermute(lax.slice_in_dim(block, 0, width, axis=dim), axis, backward)  24.4 us
    ppermute x10, waiting for transfers between devices, with_halo(): lax.ppermute(lax.slice_in_dim(block, 0, width, axis=dim), axis, backward)  16.8 us
    dot_general x6, matrix products, face_mul(): jnp.einsum('fry,fyx->frx', vectors, matrices, preferred_element_type=jnp....  9.97 us
  transfers between devices with their start and end apart: 20, of which 5 were waited for; matrix products, arithmetic and copies ran while one was open for 1% of the time, Pallas kernels for 0%

commit v1 on v0

--- a/solution.py
+++ b/solution.py
@@ -77,7 +77,7 @@
     first = precondition(resid0)
     resid1 = resid0 - apply_operator(first)
     second = precondition(resid1)
-    top = lax.psum(jnp.sum(resid1 * second, axis=(0, 2)), ("gx", "gy"))
+    top = lax.psum(lax.psum(jnp.sum(resid1 * second, axis=(0, 2)), "gy"), "gx")
     curved = apply_operator(second)
     bottom = lax.psum(jnp.sum(second * curved, axis=(0, 2)), ("gx", "gy"))
     step_len = top / bottom

time: 211 us -> 252 us (1.19)
  blocking collectives: 115 us -> 156 us
  waiting for transfers between devices: 16.9 us -> 13.1 us
    psum x1 -> x3, blocking collectives: 45.2 us -> 86.3 us  [the longest x1 47.5 us: per_device(): bottom = lax.psum(jnp.sum(second * curved, axis=(0, 2)), ('gx', 'gy'))]
    ppermute x10, waiting for transfers between devices: 16.8 us -> 13.1 us  [with_halo(): lax.ppermute(lax.slice_in_dim(block, 0, width, axis=dim), axis, backward)]
  transfers between devices with their start and end apart: 20 -> 20, of which waited for: 5 -> 4; matrix products, arithmetic and copies ran while one was open for 1% -> 0% of each run, Pallas kernels for 0% -> 0%
where the time goes in v1:
time: 252 us; the launch traced here: 251 us
  blocking collectives  156 us (62%)
  starting transfers between devices  56.1 us (22%)
  matrix products  15.6 us (6%)
  waiting for transfers between devices  13.1 us (5%)
  local copies, waits for them, and re-layouts  5.08 us (2%)
  other arithmetic  4.35 us (2%)
    all_gather x2, blocking collectives, precondition(): lax.all_gather(primal, ('gx', 'gy'), axis=0, tiled=True)  69.4 us
    psum x1, blocking collectives, per_device(): bottom = lax.psum(jnp.sum(second * curved, axis=(0, 2)), ('gx', 'gy'))  47.5 us
    psum x2, blocking collectives, per_device(): top = lax.psum(lax.psum(jnp.sum(resid1 * second, axis=(0, 2)), 'gy'), 'gx')  38.8 us
    ppermute x10, starting transfers between devices, with_halo(): lax.ppermute(lax.slice_in_dim(block, block.shape[dim] - width, None, axis...  31.7 us
    ppermute x10, starting transfers between devices, with_halo(): lax.ppermute(lax.slice_in_dim(block, 0, width, axis=dim), axis, backward)  24.4 us
    ppermute x10, waiting for transfers between devices, with_halo(): lax.ppermute(lax.slice_in_dim(block, 0, width, axis=dim), axis, backward)  13.1 us
    dot_general x6, matrix products, face_mul(): jnp.einsum('fry,fyx->frx', vectors, matrices, preferred_element_type=jnp....  9.99 us
  transfers between devices with their start and end apart: 20, of which 4 were waited for; matrix products, arithmetic and copies ran while one was open for 0% of the time, Pallas kernels for 0%

profile of v1, /device:TPU:10, one launch (start us, length us, event | category | flops | bytes accessed | tf_op | source)
XLA Modules:
  0.0 250.8 jit_solution(2361604040220817002)
XLA Ops:
  0.0 1.3 slice_bitcast_fusion.3
  1.3 3.4 %collective-permute-start = (bf16[1,192,384]{2,1,0:T(8,128)(2,1)S(1)}, bf16[1,192,384]{2,1,0:T(8,128)(2,1)S(1)}, u32[]{:S(2)}, u32[]{:S(2)}) collective-permute-start(bf16[1,192,384]{2,1,0:T(8,128)(2,1)S(1)} %get-tuple-element.21), channel_id=1, source_target_pairs={{0,2},{2,4},{4,6},{6,8},{8,10},{10,12},{12,14},{14,16},{16,18},{18... | collective-permute-start | bytes 442376 | tf_op jit(solution)/shard_map/ppermute | solution.py:12
  4.7 2.4 collective-permute-start.1
  7.2 1.3 collective-permute-start.3
  8.5 3.0 %collective-permute-start.2 = (bf16[1,192,384]{2,1,0:T(8,128)(2,1)S(1)}, bf16[1,192,384]{2,1,0:T(8,128)(2,1)S(1)}, u32[]{:S(2)}, u32[]{:S(2)}) collective-permute-start(bf16[1,192,384]{2,1,0:T(8,128)(2,1)S(1)} %get-tuple-element.24), channel_id=1, source_target_pairs={{0,1},{2,3},{4,5},{6,7},{8,9},{10,11},{12,13},{14,15},{16,17},{18,... | collective-permute-start | bytes 442376 | tf_op jit(solution)/shard_map/ppermute | solution.py:12
  11.6 0.5 multiply_bitcast_fusion
  12.1 0.8 collective-permute-done.1
  12.9 0.0 collective-permute-done.3
  12.9 0.0 collective-permute-done.2
  13.0 0.0 copy-start.1
  13.0 0.6 convolution_convert_fusion.5
  13.6 0.0 copy-done.22
  13.7 0.0 copy-done.25
  13.7 0.3 fusion.25
  14.0 34.1 %all-gather = bf16[32,4,192]{2,1,0:T(4,128)(2,1)} all-gather(bf16[1,4,192]{2,1,0:T(4,128)(2,1)S(1)} %fusion.25), channel_id=1, replica_groups=mesh['gx'=16,'gy'=2] {'gx','gy'}, dimensions={0}, use_global_device_ids=true | all-gather | bytes 50688 | tf_op jit(solution)/shard_map/all_gather | solution.py:66
  48.0 1.5 reshape.37
  49.6 1.6 fusion.14
  51.1 0.1 convolution_bitcast_fusion.5
  51.2 1.8 convolution_bitcast_fusion.1
  53.0 2.9 %convolution_convert_fusion.4 = bf16[4,192,384]{2,1,0:T(8,128)(2,1)S(1)} fusion(f32[4,192,384]{2,1,0:T(8,128)} %convolution_bitcast_fusion.1, f32[4,192,384]{2,1,0:T(8,128)} %fusion.14, bf16[1,1,4,384,384]{4,3,2,1,0:T(8,128)(2,1)S(1)} %copy-done.1, bf16[1,1,4,384,384]{4,3,2,1,0:T(8,128)(2,1)S(1)} %copy-done, f32[4]{0:T(128)} %multiply_bitcast_fusion), kind=kOutput, calls=%fused_computation.14 | convolution fusion | flops 454754304 | bytes 5308432 | tf_op jit(solution)/shard_map/fry,fyx->frx/dot_general | solution.py:21
  55.9 0.0 copy-start.46
  55.9 0.1 fusion.56
  56.0 3.5 %collective-permute-start.4 = (bf16[1,192,384]{2,1,0:T(8,128)(2,1)S(1)}, bf16[1,192,384]{2,1,0:T(8,128)(2,1)S(1)}, u32[]{:S(2)}, u32[]{:S(2)}) collective-permute-start(bf16[1,192,384]{2,1,0:T(8,128)(2,1)S(1)} %get-tuple-element.17), channel_id=1, source_target_pairs={{0,2},{2,4},{4,6},{6,8},{8,10},{10,12},{12,14},{14,16},{16,18},{18... | collective-permute-start | bytes 442376 | tf_op jit(solution)/shard_map/ppermute | solution.py:12
  59.6 1.3 collective-permute-start.7
  60.9 3.0 %collective-permute-start.6 = (bf16[1,192,384]{2,1,0:T(8,128)(2,1)S(1)}, bf16[1,192,384]{2,1,0:T(8,128)(2,1)S(1)}, u32[]{:S(2)}, u32[]{:S(2)}) collective-permute-start(bf16[1,192,384]{2,1,0:T(8,128)(2,1)S(1)} %get-tuple-element.19), channel_id=1, source_target_pairs={{0,1},{2,3},{4,5},{6,7},{8,9},{10,11},{12,13},{14,15},{16,17},{18,... | collective-permute-start | bytes 442376 | tf_op jit(solution)/shard_map/ppermute | solution.py:12
  63.9 4.6 %collective-permute-start.5 = (bf16[1,192,384]{2,1,0:T(8,128)(2,1)S(1)}, bf16[1,192,384]{2,1,0:T(8,128)(2,1)S(1)}, u32[]{:S(2)}, u32[]{:S(2)}) collective-permute-start(bf16[1,192,384]{2,1,0:T(8,128)(2,1)S(1)} %get-tuple-element.20), channel_id=1, source_target_pairs={{2,0},{4,2},{6,4},{8,6},{10,8},{12,10},{14,12},{16,14},{18,16},{20... | collective-permute-start | bytes 442376 | tf_op jit(solution)/shard_map/ppermute | solution.py:15
  68.5 0.0 collective-permute-done.4
  68.5 0.0 collective-permute-done.7
  68.6 3.3 %collective-permute-done.5 = bf16[1,192,384]{2,1,0:T(8,128)(2,1)S(1)} collective-permute-done((bf16[1,192,384]{2,1,0:T(8,128)(2,1)S(1)}, bf16[1,192,384]{2,1,0:T(8,128)(2,1)S(1)}, u32[]{:S(2)}, u32[]{:S(2)}) %collective-permute-start.5) | collective-permute-done | bytes 147488 | tf_op jit(solution)/shard_map/ppermute | solution.py:15
  71.8 0.5 convolution_convert_fusion.3
  72.4 0.1 copy-done.34
  72.5 0.1 fusion.55
  72.6 3.5 %collective-permute-start.8 = (bf16[1,192,384]{2,1,0:T(8,128)(2,1)S(1)}, bf16[1,192,384]{2,1,0:T(8,128)(2,1)S(1)}, u32[]{:S(2)}, u32[]{:S(2)}) collective-permute-start(bf16[1,192,384]{2,1,0:T(8,128)(2,1)S(1)} %get-tuple-element.13), channel_id=1, source_target_pairs={{0,2},{2,4},{4,6},{6,8},{8,10},{10,12},{12,14},{14,16},{16,18},{18... | collective-permute-start | bytes 442376 | tf_op jit(solution)/shard_map/ppermute | solution.py:12
  76.1 1.3 collective-permute-start.11
  77.4 3.0 %collective-permute-start.10 = (bf16[1,192,384]{2,1,0:T(8,128)(2,1)S(1)}, bf16[1,192,384]{2,1,0:T(8,128)(2,1)S(1)}, u32[]{:S(2)}, u32[]{:S(2)}) collective-permute-start(bf16[1,192,384]{2,1,0:T(8,128)(2,1)S(1)} %get-tuple-element.15), channel_id=1, source_target_pairs={{0,1},{2,3},{4,5},{6,7},{8,9},{10,11},{12,13},{14,15},{16,17},{18,... | collective-permute-start | bytes 442376 | tf_op jit(solution)/shard_map/ppermute | solution.py:12
  80.4 3.6 %collective-permute-start.9 = (bf16[1,192,384]{2,1,0:T(8,128)(2,1)S(1)}, bf16[1,192,384]{2,1,0:T(8,128)(2,1)S(1)}, u32[]{:S(2)}, u32[]{:S(2)}) collective-permute-start(bf16[1,192,384]{2,1,0:T(8,128)(2,1)S(1)} %get-tuple-element.16), channel_id=1, source_target_pairs={{2,0},{4,2},{6,4},{8,6},{10,8},{12,10},{14,12},{16,14},{18,16},{20... | collective-permute-start | bytes 442376 | tf_op jit(solution)/shard_map/ppermute | solution.py:15
  84.1 5.0 %collective-permute-done.9 = bf16[1,192,384]{2,1,0:T(8,128)(2,1)S(1)} collective-permute-done((bf16[1,192,384]{2,1,0:T(8,128)(2,1)S(1)}, bf16[1,192,384]{2,1,0:T(8,128)(2,1)S(1)}, u32[]{:S(2)}, u32[]{:S(2)}) %collective-permute-start.9) | collective-permute-done | bytes 147488 | tf_op jit(solution)/shard_map/ppermute | solution.py:15
  89.2 0.6 convolution_convert_fusion.2
  89.9 0.3 fusion.24
  90.2 1.6 fusion.10
  91.7 35.3 %all-gather.1 = bf16[32,4,192]{2,1,0:T(4,128)(2,1)S(1)} all-gather(bf16[1,4,192]{2,1,0:T(4,128)(2,1)S(1)} %fusion.24), channel_id=1, replica_groups=mesh['gx'=16,'gy'=2] {'gx','gy'}, dimensions={0}, use_global_device_ids=true | all-gather | bytes 50688 | tf_op jit(solution)/shard_map/all_gather | solution.py:66
  127.1 0.1 convolution_bitcast_fusion.4
  127.3 1.8 convolution_bitcast_fusion
  129.1 2.9 %convolution_convert_fusion.1 = bf16[4,192,384]{2,1,0:T(8,128)(2,1)S(1)} fusion(f32[4,192,384]{2,1,0:T(8,128)} %convolution_bitcast_fusion, f32[4,192,384]{2,1,0:T(8,128)} %fusion.10, bf16[1,1,4,384,384]{4,3,2,1,0:T(8,128)(2,1)S(1)} %copy-done.1, bf16[1,1,4,384,384]{4,3,2,1,0:T(8,128)(2,1)S(1)} %copy-done, f32[4]{0:T(128)} %multiply_bitcast_fusion), kind=kOutput, calls=%fused_computation.11 | convolution fusion | flops 454754304 | bytes 5308432 | tf_op jit(solution)/shard_map/fry,fyx->frx/dot_general | solution.py:21
  131.9 0.0 copy-start.47
  132.0 0.1 fusion.54
  132.0 2.1 collective-permute-start.12
  134.1 1.3 collective-permute-start.15
  135.4 3.0 %collective-permute-start.14 = (bf16[1,192,384]{2,1,0:T(8,128)(2,1)S(1)}, bf16[1,192,384]{2,1,0:T(8,128)(2,1)S(1)}, u32[]{:S(2)}, u32[]{:S(2)}) collective-permute-start(bf16[1,192,384]{2,1,0:T(8,128)(2,1)S(1)} %get-tuple-element.11), channel_id=1, source_target_pairs={{0,1},{2,3},{4,5},{6,7},{8,9},{10,11},{12,13},{14,15},{16,17},{18,... | collective-permute-start | bytes 442376 | tf_op jit(solution)/shard_map/ppermute | solution.py:12
  138.4 3.9 %collective-permute-start.13 = (bf16[1,192,384]{2,1,0:T(8,128)(2,1)S(1)}, bf16[1,192,384]{2,1,0:T(8,128)(2,1)S(1)}, u32[]{:S(2)}, u32[]{:S(2)}) collective-permute-start(bf16[1,192,384]{2,1,0:T(8,128)(2,1)S(1)} %get-tuple-element.12), channel_id=1, source_target_pairs={{2,0},{4,2},{6,4},{8,6},{10,8},{12,10},{14,12},{16,14},{18,16},{20... | collective-permute-start | bytes 442376 | tf_op jit(solution)/shard_map/ppermute | solution.py:15
  142.4 3.9 %collective-permute-done.13 = bf16[1,192,384]{2,1,0:T(8,128)(2,1)S(1)} collective-permute-done((bf16[1,192,384]{2,1,0:T(8,128)(2,1)S(1)}, bf16[1,192,384]{2,1,0:T(8,128)(2,1)S(1)}, u32[]{:S(2)}, u32[]{:S(2)}) %collective-permute-start.13) | collective-permute-done | bytes 147488 | tf_op jit(solution)/shard_map/ppermute | solution.py:15
  146.4 0.5 convolution_convert_fusion
  147.0 0.8 copy-done.6
  147.8 0.8 fusion.53
  148.7 2.7 %collective-permute-start.16 = (bf16[1,192,384]{2,1,0:T(8,128)(2,1)}, bf16[1,192,384]{2,1,0:T(8,128)(2,1)}, u32[]{:S(2)}, u32[]{:S(2)}) collective-permute-start(bf16[1,192,384]{2,1,0:T(8,128)(2,1)} %get-tuple-element.5), channel_id=1, source_target_pairs={{0,2},{2,4},{4,6},{6,8},{8,10},{10,12},{12,14},{14,16},{16,18},{18... | collective-permute-start | bytes 442376 | tf_op jit(solution)/shard_map/ppermute | solution.py:12
  151.4 1.3 collective-permute-start.19
  152.7 4.3 %collective-permute-start.18 = (bf16[1,192,384]{2,1,0:T(8,128)(2,1)}, bf16[1,192,384]{2,1,0:T(8,128)(2,1)}, u32[]{:S(2)}, u32[]{:S(2)}) collective-permute-start(bf16[1,192,384]{2,1,0:T(8,128)(2,1)} %get-tuple-element.7), channel_id=1, source_target_pairs={{0,1},{2,3},{4,5},{6,7},{8,9},{10,11},{12,13},{14,15},{16,17},{18,... | collective-permute-start | bytes 442376 | tf_op jit(solution)/shard_map/ppermute | solution.py:12
  157.0 3.3 %collective-permute-start.17 = (bf16[1,192,384]{2,1,0:T(8,128)(2,1)}, bf16[1,192,384]{2,1,0:T(8,128)(2,1)}, u32[]{:S(2)}, u32[]{:S(2)}) collective-permute-start(bf16[1,192,384]{2,1,0:T(8,128)(2,1)} %get-tuple-element.8), channel_id=1, source_target_pairs={{2,0},{4,2},{6,4},{8,6},{10,8},{12,10},{14,12},{16,14},{18,16},{20... | collective-permute-start | bytes 442376 | tf_op jit(solution)/shard_map/ppermute | solution.py:15
  160.5 0.6 multiply_reduce_fusion.1
  161.1 2.5 psum.21
  163.6 36.3 %psum.22 = f32[192]{0:T(256)S(1)} all-reduce(f32[192]{0:T(256)S(1)} %psum.21), channel_id=1, replica_groups=mesh['gx'=16,'gy'=2] {'gx'}, use_global_device_ids=true, to_apply=%region_2.0 | all-reduce | flops 192 | bytes 1536 | tf_op jit(solution)/shard_map/psum | solution.py:80
  200.0 2.0 multiply_reduce_fusion
  202.0 47.5 %psum.23 = f32[192]{0:T(256)S(1)} all-reduce(f32[192]{0:T(256)S(1)} %multiply_reduce_fusion), channel_id=1, replica_groups=mesh['gx'=16,'gy'=2] {'gx','gy'}, use_global_device_ids=true, to_apply=%region_4.0 | all-reduce | flops 192 | bytes 1536 | tf_op jit(solution)/shard_map/psum | solution.py:82
  249.6 1.2 fusion.30
  (106 shorter events, 0.3 us)
Async XLA Ops:
  0.0 12.9 %copy-start = (bf16[1,1,4,384,384]{4,3,2,1,0:T(8,128)(2,1)S(1)}, bf16[1,1,4,384,384]{4,3,2,1,0:T(8,128)(2,1)}, u32[]{:S(2)}) copy-start(bf16[1,1,4,384,384]{4,3,2,1,0:T(8,128)(2,1)} %param.9) | copy-start | bytes 3538948
  0.0 13.0 %copy-start.2 = (bf16[1,1,4,192,384]{4,3,2,1,0:T(8,128)(2,1)S(1)}, bf16[1,1,4,192,384]{4,3,2,1,0:T(8,128)(2,1)}, u32[]{:S(2)}) copy-start(bf16[1,1,4,192,384]{4,3,2,1,0:T(8,128)(2,1)} %param.7) | copy-start | bytes 1769476
  0.0 11.5 %copy-start.48 = (s32[1,1,4]{2,1,0:T(1,128)S(1)}, s32[1,1,4]{2,1,0:T(1,128)}, u32[]{:S(2)}) copy-start(s32[1,1,4]{2,1,0:T(1,128)} %param.13) | copy-start | bytes 52
  1.3 10.8 %collective-permute-start = (bf16[1,192,384]{2,1,0:T(8,128)(2,1)S(1)}, bf16[1,192,384]{2,1,0:T(8,128)(2,1)S(1)}, u32[]{:S(2)}, u32[]{:S(2)}) collective-permute-start(bf16[1,192,384]{2,1,0:T(8,128)(2,1)S(1)} %get-tuple-element.21), channel_id=1, source_target_pairs={{0,2},{2,4},{4,6},{6,8},{8,10},{10,12},{12,14},{14,16},{16,18},{18... | collective-permute-start | bytes 442376 | tf_op jit(solution)/shard_map/ppermute | solution.py:12
  4.7 8.2 %collective-permute-start.1 = (bf16[1,192,384]{2,1,0:T(8,128)(2,1)S(1)}, bf16[1,192,384]{2,1,0:T(8,128)(2,1)S(1)}, u32[]{:S(2)}, u32[]{:S(2)}) collective-permute-start(bf16[1,192,384]{2,1,0:T(8,128)(2,1)S(1)} %get-tuple-element.22), channel_id=1, source_target_pairs={{2,0},{4,2},{6,4},{8,6},{10,8},{12,10},{14,12},{16,14},{18,16},{20... | collective-permute-start | bytes 442376 | tf_op jit(solution)/shard_map/ppermute | solution.py:15
  7.2 5.7 %collective-permute-start.3 = (bf16[1,192,384]{2,1,0:T(8,128)(2,1)S(1)}, bf16[1,192,384]{2,1,0:T(8,128)(2,1)S(1)}, u32[]{:S(2)}, u32[]{:S(2)}) collective-permute-start(bf16[1,192,384]{2,1,0:T(8,128)(2,1)S(1)} %get-tuple-element.23), channel_id=1, source_target_pairs={{1,0},{3,2},{5,4},{7,6},{9,8},{11,10},{13,12},{15,14},{17,16},{19,... | collective-permute-start | bytes 442376 | tf_op jit(solution)/shard_map/ppermute | solution.py:15
  8.5 4.5 %collective-permute-start.2 = (bf16[1,192,384]{2,1,0:T(8,128)(2,1)S(1)}, bf16[1,192,384]{2,1,0:T(8,128)(2,1)S(1)}, u32[]{:S(2)}, u32[]{:S(2)}) collective-permute-start(bf16[1,192,384]{2,1,0:T(8,128)(2,1)S(1)} %get-tuple-element.24), channel_id=1, source_target_pairs={{0,1},{2,3},{4,5},{6,7},{8,9},{10,11},{12,13},{14,15},{16,17},{18,... | collective-permute-start | bytes 442376 | tf_op jit(solution)/shard_map/ppermute | solution.py:12
  12.1 1.6 copy-start.45
  12.1 1.5 copy-start.16
  13.0 36.6 %copy-start.1 = (bf16[1,1,4,384,384]{4,3,2,1,0:T(8,128)(2,1)S(1)}, bf16[1,1,4,384,384]{4,3,2,1,0:T(8,128)(2,1)}, u32[]{:S(2)}) copy-start(bf16[1,1,4,384,384]{4,3,2,1,0:T(8,128)(2,1)} %param.10) | copy-start | bytes 3538948
  49.6 1.6 copy-start.15
  49.6 1.6 copy-start.44
  55.9 15.9 %copy-start.46 = (bf16[1,1,4,384,384]{4,3,2,1,0:T(8,128)(2,1)S(1)}, bf16[1,1,4,384,384]{4,3,2,1,0:T(8,128)(2,1)}, u32[]{:S(2)}) copy-start(bf16[1,1,4,384,384]{4,3,2,1,0:T(8,128)(2,1)} %param.8) | copy-start | bytes 3538948
  56.0 12.5 %collective-permute-start.4 = (bf16[1,192,384]{2,1,0:T(8,128)(2,1)S(1)}, bf16[1,192,384]{2,1,0:T(8,128)(2,1)S(1)}, u32[]{:S(2)}, u32[]{:S(2)}) collective-permute-start(bf16[1,192,384]{2,1,0:T(8,128)(2,1)S(1)} %get-tuple-element.17), channel_id=1, source_target_pairs={{0,2},{2,4},{4,6},{6,8},{8,10},{10,12},{12,14},{14,16},{16,18},{18... | collective-permute-start | bytes 442376 | tf_op jit(solution)/shard_map/ppermute | solution.py:12
  59.6 9.0 %collective-permute-start.7 = (bf16[1,192,384]{2,1,0:T(8,128)(2,1)S(1)}, bf16[1,192,384]{2,1,0:T(8,128)(2,1)S(1)}, u32[]{:S(2)}, u32[]{:S(2)}) collective-permute-start(bf16[1,192,384]{2,1,0:T(8,128)(2,1)S(1)} %get-tuple-element.18), channel_id=1, source_target_pairs={{1,0},{3,2},{5,4},{7,6},{9,8},{11,10},{13,12},{15,14},{17,16},{19,... | collective-permute-start | bytes 442376 | tf_op jit(solution)/shard_map/ppermute | solution.py:15
  60.9 7.7 %collective-permute-start.6 = (bf16[1,192,384]{2,1,0:T(8,128)(2,1)S(1)}, bf16[1,192,384]{2,1,0:T(8,128)(2,1)S(1)}, u32[]{:S(2)}, u32[]{:S(2)}) collective-permute-start(bf16[1,192,384]{2,1,0:T(8,128)(2,1)S(1)} %get-tuple-element.19), channel_id=1, source_target_pairs={{0,1},{2,3},{4,5},{6,7},{8,9},{10,11},{12,13},{14,15},{16,17},{18,... | collective-permute-start | bytes 442376 | tf_op jit(solution)/shard_map/ppermute | solution.py:12
  63.9 7.9 %collective-permute-start.5 = (bf16[1,192,384]{2,1,0:T(8,128)(2,1)S(1)}, bf16[1,192,384]{2,1,0:T(8,128)(2,1)S(1)}, u32[]{:S(2)}, u32[]{:S(2)}) collective-permute-start(bf16[1,192,384]{2,1,0:T(8,128)(2,1)S(1)} %get-tuple-element.20), channel_id=1, source_target_pairs={{2,0},{4,2},{6,4},{8,6},{10,8},{12,10},{14,12},{16,14},{18,16},{20... | collective-permute-start | bytes 442376 | tf_op jit(solution)/shard_map/ppermute | solution.py:15
  68.5 3.8 %copy-start.28 = (bf16[1,192,384]{2,1,0:T(8,128)(2,1)}, bf16[1,192,384]{2,1,0:T(8,128)(2,1)S(1)}, u32[]{:S(2)}) copy-start(bf16[1,192,384]{2,1,0:T(8,128)(2,1)S(1)} %collective-permute-done.4) | copy-start | bytes 442372
  68.6 3.8 %copy-start.30 = (bf16[1,192,384]{2,1,0:T(8,128)(2,1)}, bf16[1,192,384]{2,1,0:T(8,128)(2,1)S(1)}, u32[]{:S(2)}) copy-start(bf16[1,192,384]{2,1,0:T(8,128)(2,1)S(1)} %collective-permute-done.7) | copy-start | bytes 442372
  68.6 3.8 %copy-start.32 = (bf16[1,192,384]{2,1,0:T(8,128)(2,1)}, bf16[1,192,384]{2,1,0:T(8,128)(2,1)S(1)}, u32[]{:S(2)}) copy-start(bf16[1,192,384]{2,1,0:T(8,128)(2,1)S(1)} %collective-permute-done.6) | copy-start | bytes 442372
  72.5 17.3 %copy-start.4 = (bf16[4,192,384]{2,1,0:T(8,128)(2,1)}, bf16[4,192,384]{2,1,0:T(8,128)(2,1)S(1)}, u32[]{:S(2)}) copy-start(bf16[4,192,384]{2,1,0:T(8,128)(2,1)S(1)} %convolution_convert_fusion.3) | copy-start | bytes 1769476
  72.5 16.7 %copy-start.17 = (bf16[1,192,384]{2,1,0:T(8,128)(2,1)S(1)}, bf16[1,192,384]{2,1,0:T(8,128)(2,1)}, u32[]{:S(2)}) copy-start(bf16[1,192,384]{2,1,0:T(8,128)(2,1)} %copy-done.16) | copy-start | bytes 442372
  72.5 16.7 %copy-start.20 = (bf16[1,192,384]{2,1,0:T(8,128)(2,1)S(1)}, bf16[1,192,384]{2,1,0:T(8,128)(2,1)}, u32[]{:S(2)}) copy-start(bf16[1,192,384]{2,1,0:T(8,128)(2,1)} %copy-done.19) | copy-start | bytes 442372
  72.5 16.7 %copy-start.23 = (bf16[1,192,384]{2,1,0:T(8,128)(2,1)S(1)}, bf16[1,192,384]{2,1,0:T(8,128)(2,1)}, u32[]{:S(2)}) copy-start(bf16[1,192,384]{2,1,0:T(8,128)(2,1)} %copy-done.22) | copy-start | bytes 442372
  72.5 16.7 %copy-start.26 = (bf16[1,192,384]{2,1,0:T(8,128)(2,1)S(1)}, bf16[1,192,384]{2,1,0:T(8,128)(2,1)}, u32[]{:S(2)}) copy-start(bf16[1,192,384]{2,1,0:T(8,128)(2,1)} %copy-done.25) | copy-start | bytes 442372
  72.6 11.5 %collective-permute-start.8 = (bf16[1,192,384]{2,1,0:T(8,128)(2,1)S(1)}, bf16[1,192,384]{2,1,0:T(8,128)(2,1)S(1)}, u32[]{:S(2)}, u32[]{:S(2)}) collective-permute-start(bf16[1,192,384]{2,1,0:T(8,128)(2,1)S(1)} %get-tuple-element.13), channel_id=1, source_target_pairs={{0,2},{2,4},{4,6},{6,8},{8,10},{10,12},{12,14},{14,16},{16,18},{18... | collective-permute-start | bytes 442376 | tf_op jit(solution)/shard_map/ppermute | solution.py:12
  76.1 8.0 %collective-permute-start.11 = (bf16[1,192,384]{2,1,0:T(8,128)(2,1)S(1)}, bf16[1,192,384]{2,1,0:T(8,128)(2,1)S(1)}, u32[]{:S(2)}, u32[]{:S(2)}) collective-permute-start(bf16[1,192,384]{2,1,0:T(8,128)(2,1)S(1)} %get-tuple-element.14), channel_id=1, source_target_pairs={{1,0},{3,2},{5,4},{7,6},{9,8},{11,10},{13,12},{15,14},{17,16},{19,... | collective-permute-start | bytes 442376 | tf_op jit(solution)/shard_map/ppermute | solution.py:15
  77.4 6.7 %collective-permute-start.10 = (bf16[1,192,384]{2,1,0:T(8,128)(2,1)S(1)}, bf16[1,192,384]{2,1,0:T(8,128)(2,1)S(1)}, u32[]{:S(2)}, u32[]{:S(2)}) collective-permute-start(bf16[1,192,384]{2,1,0:T(8,128)(2,1)S(1)} %get-tuple-element.15), channel_id=1, source_target_pairs={{0,1},{2,3},{4,5},{6,7},{8,9},{10,11},{12,13},{14,15},{16,17},{18,... | collective-permute-start | bytes 442376 | tf_op jit(solution)/shard_map/ppermute | solution.py:12
  80.4 8.7 %collective-permute-start.9 = (bf16[1,192,384]{2,1,0:T(8,128)(2,1)S(1)}, bf16[1,192,384]{2,1,0:T(8,128)(2,1)S(1)}, u32[]{:S(2)}, u32[]{:S(2)}) collective-permute-start(bf16[1,192,384]{2,1,0:T(8,128)(2,1)S(1)} %get-tuple-element.16), channel_id=1, source_target_pairs={{2,0},{4,2},{6,4},{8,6},{10,8},{12,10},{14,12},{16,14},{18,16},{20... | collective-permute-start | bytes 442376 | tf_op jit(solution)/shard_map/ppermute | solution.py:15
  84.1 5.8 %copy-start.36 = (bf16[1,192,384]{2,1,0:T(8,128)(2,1)}, bf16[1,192,384]{2,1,0:T(8,128)(2,1)S(1)}, u32[]{:S(2)}) copy-start(bf16[1,192,384]{2,1,0:T(8,128)(2,1)S(1)} %collective-permute-done.8) | copy-start | bytes 442372
  84.1 5.8 %copy-start.38 = (bf16[1,192,384]{2,1,0:T(8,128)(2,1)}, bf16[1,192,384]{2,1,0:T(8,128)(2,1)S(1)}, u32[]{:S(2)}) copy-start(bf16[1,192,384]{2,1,0:T(8,128)(2,1)S(1)} %collective-permute-done.11) | copy-start | bytes 442372
  84.1 5.8 %copy-start.40 = (bf16[1,192,384]{2,1,0:T(8,128)(2,1)}, bf16[1,192,384]{2,1,0:T(8,128)(2,1)S(1)}, u32[]{:S(2)}) copy-start(bf16[1,192,384]{2,1,0:T(8,128)(2,1)S(1)} %collective-permute-done.10) | copy-start | bytes 442372
  131.9 14.4 %copy-start.47 = (bf16[1,1,4,384,384]{4,3,2,1,0:T(8,128)(2,1)S(1)}, bf16[1,1,4,384,384]{4,3,2,1,0:T(8,128)(2,1)}, u32[]{:S(2)}) copy-start(bf16[1,1,4,384,384]{4,3,2,1,0:T(8,128)(2,1)} %param.8) | copy-start | bytes 3538948
  132.0 10.3 %collective-permute-start.12 = (bf16[1,192,384]{2,1,0:T(8,128)(2,1)S(1)}, bf16[1,192,384]{2,1,0:T(8,128)(2,1)S(1)}, u32[]{:S(2)}, u32[]{:S(2)}) collective-permute-start(bf16[1,192,384]{2,1,0:T(8,128)(2,1)S(1)} %get-tuple-element.9), channel_id=1, source_target_pairs={{0,2},{2,4},{4,6},{6,8},{8,10},{10,12},{12,14},{14,16},{16,18},{18... | collective-permute-start | bytes 442376 | tf_op jit(solution)/shard_map/ppermute | solution.py:12
  134.1 8.3 %collective-permute-start.15 = (bf16[1,192,384]{2,1,0:T(8,128)(2,1)S(1)}, bf16[1,192,384]{2,1,0:T(8,128)(2,1)S(1)}, u32[]{:S(2)}, u32[]{:S(2)}) collective-permute-start(bf16[1,192,384]{2,1,0:T(8,128)(2,1)S(1)} %get-tuple-element.10), channel_id=1, source_target_pairs={{1,0},{3,2},{5,4},{7,6},{9,8},{11,10},{13,12},{15,14},{17,16},{19,... | collective-permute-start | bytes 442376 | tf_op jit(solution)/shard_map/ppermute | solution.py:15
  135.4 7.0 %collective-permute-start.14 = (bf16[1,192,384]{2,1,0:T(8,128)(2,1)S(1)}, bf16[1,192,384]{2,1,0:T(8,128)(2,1)S(1)}, u32[]{:S(2)}, u32[]{:S(2)}) collective-permute-start(bf16[1,192,384]{2,1,0:T(8,128)(2,1)S(1)} %get-tuple-element.11), channel_id=1, source_target_pairs={{0,1},{2,3},{4,5},{6,7},{8,9},{10,11},{12,13},{14,15},{16,17},{18,... | collective-permute-start | bytes 442376 | tf_op jit(solution)/shard_map/ppermute | solution.py:12
  138.4 7.9 %collective-permute-start.13 = (bf16[1,192,384]{2,1,0:T(8,128)(2,1)S(1)}, bf16[1,192,384]{2,1,0:T(8,128)(2,1)S(1)}, u32[]{:S(2)}, u32[]{:S(2)}) collective-permute-start(bf16[1,192,384]{2,1,0:T(8,128)(2,1)S(1)} %get-tuple-element.12), channel_id=1, source_target_pairs={{2,0},{4,2},{6,4},{8,6},{10,8},{12,10},{14,12},{16,14},{18,16},{20... | collective-permute-start | bytes 442376 | tf_op jit(solution)/shard_map/ppermute | solution.py:15
  142.4 18.0 %copy-start.7 = (bf16[1,192,384]{2,1,0:T(8,128)(2,1)}, bf16[1,192,384]{2,1,0:T(8,128)(2,1)S(1)}, u32[]{:S(2)}) copy-start(bf16[1,192,384]{2,1,0:T(8,128)(2,1)S(1)} %collective-permute-done.12) | copy-start | bytes 442372
  142.4 18.0 %copy-start.9 = (bf16[1,192,384]{2,1,0:T(8,128)(2,1)}, bf16[1,192,384]{2,1,0:T(8,128)(2,1)S(1)}, u32[]{:S(2)}) copy-start(bf16[1,192,384]{2,1,0:T(8,128)(2,1)S(1)} %collective-permute-done.15) | copy-start | bytes 442372
  142.4 18.0 %copy-start.11 = (bf16[1,192,384]{2,1,0:T(8,128)(2,1)}, bf16[1,192,384]{2,1,0:T(8,128)(2,1)S(1)}, u32[]{:S(2)}) copy-start(bf16[1,192,384]{2,1,0:T(8,128)(2,1)S(1)} %collective-permute-done.14) | copy-start | bytes 442372
  146.4 14.1 %copy-start.13 = (bf16[1,192,384]{2,1,0:T(8,128)(2,1)}, bf16[1,192,384]{2,1,0:T(8,128)(2,1)S(1)}, u32[]{:S(2)}) copy-start(bf16[1,192,384]{2,1,0:T(8,128)(2,1)S(1)} %collective-permute-done.13) | copy-start | bytes 442372
  146.4 14.1 %copy-start.18 = (bf16[1,192,384]{2,1,0:T(8,128)(2,1)S(1)}, bf16[1,192,384]{2,1,0:T(8,128)(2,1)}, u32[]{:S(2)}) copy-start(bf16[1,192,384]{2,1,0:T(8,128)(2,1)} %copy-done.16) | copy-start | bytes 442372
  146.4 14.1 %copy-start.21 = (bf16[1,192,384]{2,1,0:T(8,128)(2,1)S(1)}, bf16[1,192,384]{2,1,0:T(8,128)(2,1)}, u32[]{:S(2)}) copy-start(bf16[1,192,384]{2,1,0:T(8,128)(2,1)} %copy-done.19) | copy-start | bytes 442372
  146.4 14.1 %copy-start.24 = (bf16[1,192,384]{2,1,0:T(8,128)(2,1)S(1)}, bf16[1,192,384]{2,1,0:T(8,128)(2,1)}, u32[]{:S(2)}) copy-start(bf16[1,192,384]{2,1,0:T(8,128)(2,1)} %copy-done.22) | copy-start | bytes 442372
  146.4 14.1 %copy-start.27 = (bf16[1,192,384]{2,1,0:T(8,128)(2,1)S(1)}, bf16[1,192,384]{2,1,0:T(8,128)(2,1)}, u32[]{:S(2)}) copy-start(bf16[1,192,384]{2,1,0:T(8,128)(2,1)} %copy-done.25) | copy-start | bytes 442372
  146.4 14.1 %copy-start.37 = (bf16[1,192,384]{2,1,0:T(8,128)(2,1)S(1)}, bf16[1,192,384]{2,1,0:T(8,128)(2,1)}, u32[]{:S(2)}) copy-start(bf16[1,192,384]{2,1,0:T(8,128)(2,1)} %copy-done.36) | copy-start | bytes 442372
  146.4 14.1 %copy-start.39 = (bf16[1,192,384]{2,1,0:T(8,128)(2,1)S(1)}, bf16[1,192,384]{2,1,0:T(8,128)(2,1)}, u32[]{:S(2)}) copy-start(bf16[1,192,384]{2,1,0:T(8,128)(2,1)} %copy-done.38) | copy-start | bytes 442372
  146.4 14.1 %copy-start.41 = (bf16[1,192,384]{2,1,0:T(8,128)(2,1)S(1)}, bf16[1,192,384]{2,1,0:T(8,128)(2,1)}, u32[]{:S(2)}) copy-start(bf16[1,192,384]{2,1,0:T(8,128)(2,1)} %copy-done.40) | copy-start | bytes 442372
  146.4 14.1 %copy-start.43 = (bf16[1,192,384]{2,1,0:T(8,128)(2,1)S(1)}, bf16[1,192,384]{2,1,0:T(8,128)(2,1)}, u32[]{:S(2)}) copy-start(bf16[1,192,384]{2,1,0:T(8,128)(2,1)} %copy-done.42) | copy-start | bytes 442372
  147.0 0.8 copy-start.6
  147.8 12.7 %copy-start.3 = (bf16[1,1,4,192,384]{4,3,2,1,0:T(8,128)(2,1)S(1)}, bf16[1,1,4,192,384]{4,3,2,1,0:T(8,128)(2,1)}, u32[]{:S(2)}) copy-start(bf16[1,1,4,192,384]{4,3,2,1,0:T(8,128)(2,1)} %param.7) | copy-start | bytes 1769476
  147.8 12.7 %copy-start.5 = (bf16[4,192,384]{2,1,0:T(8,128)(2,1)S(1)}, bf16[4,192,384]{2,1,0:T(8,128)(2,1)}, u32[]{:S(2)}) copy-start(bf16[4,192,384]{2,1,0:T(8,128)(2,1)} %copy-done.4) | copy-start | bytes 1769476
  148.7 51.2 %collective-permute-start.16 = (bf16[1,192,384]{2,1,0:T(8,128)(2,1)}, bf16[1,192,384]{2,1,0:T(8,128)(2,1)}, u32[]{:S(2)}, u32[]{:S(2)}) collective-permute-start(bf16[1,192,384]{2,1,0:T(8,128)(2,1)} %get-tuple-element.5), channel_id=1, source_target_pairs={{0,2},{2,4},{4,6},{6,8},{8,10},{10,12},{12,14},{14,16},{16,18},{18... | collective-permute-start | bytes 442376 | tf_op jit(solution)/shard_map/ppermute | solution.py:12
  151.4 48.5 %collective-permute-start.19 = (bf16[1,192,384]{2,1,0:T(8,128)(2,1)}, bf16[1,192,384]{2,1,0:T(8,128)(2,1)}, u32[]{:S(2)}, u32[]{:S(2)}) collective-permute-start(bf16[1,192,384]{2,1,0:T(8,128)(2,1)} %get-tuple-element.6), channel_id=1, source_target_pairs={{1,0},{3,2},{5,4},{7,6},{9,8},{11,10},{13,12},{15,14},{17,16},{19,... | collective-permute-start | bytes 442376 | tf_op jit(solution)/shard_map/ppermute | solution.py:15
  152.7 47.2 %collective-permute-start.18 = (bf16[1,192,384]{2,1,0:T(8,128)(2,1)}, bf16[1,192,384]{2,1,0:T(8,128)(2,1)}, u32[]{:S(2)}, u32[]{:S(2)}) collective-permute-start(bf16[1,192,384]{2,1,0:T(8,128)(2,1)} %get-tuple-element.7), channel_id=1, source_target_pairs={{0,1},{2,3},{4,5},{6,7},{8,9},{10,11},{12,13},{14,15},{16,17},{18,... | collective-permute-start | bytes 442376 | tf_op jit(solution)/shard_map/ppermute | solution.py:12
  157.0 42.9 %collective-permute-start.17 = (bf16[1,192,384]{2,1,0:T(8,128)(2,1)}, bf16[1,192,384]{2,1,0:T(8,128)(2,1)}, u32[]{:S(2)}, u32[]{:S(2)}) collective-permute-start(bf16[1,192,384]{2,1,0:T(8,128)(2,1)} %get-tuple-element.8), channel_id=1, source_target_pairs={{2,0},{4,2},{6,4},{8,6},{10,8},{12,10},{14,12},{16,14},{18,16},{20... | collective-permute-start | bytes 442376 | tf_op jit(solution)/shard_map/ppermute | solution.py:15
  199.9 49.6 %copy-start.8 = (bf16[1,192,384]{2,1,0:T(8,128)(2,1)S(1)}, bf16[1,192,384]{2,1,0:T(8,128)(2,1)}, u32[]{:S(2)}) copy-start(bf16[1,192,384]{2,1,0:T(8,128)(2,1)} %copy-done.7) | copy-start | bytes 442372
  199.9 49.6 %copy-start.10 = (bf16[1,192,384]{2,1,0:T(8,128)(2,1)S(1)}, bf16[1,192,384]{2,1,0:T(8,128)(2,1)}, u32[]{:S(2)}) copy-start(bf16[1,192,384]{2,1,0:T(8,128)(2,1)} %copy-done.9) | copy-start | bytes 442372
  199.9 49.7 %copy-start.12 = (bf16[1,192,384]{2,1,0:T(8,128)(2,1)S(1)}, bf16[1,192,384]{2,1,0:T(8,128)(2,1)}, u32[]{:S(2)}) copy-start(bf16[1,192,384]{2,1,0:T(8,128)(2,1)} %copy-done.11) | copy-start | bytes 442372
  199.9 49.7 %copy-start.14 = (bf16[1,192,384]{2,1,0:T(8,128)(2,1)S(1)}, bf16[1,192,384]{2,1,0:T(8,128)(2,1)}, u32[]{:S(2)}) copy-start(bf16[1,192,384]{2,1,0:T(8,128)(2,1)} %copy-done.13) | copy-start | bytes 442372
  199.9 49.7 %copy-start.29 = (bf16[1,192,384]{2,1,0:T(8,128)(2,1)S(1)}, bf16[1,192,384]{2,1,0:T(8,128)(2,1)}, u32[]{:S(2)}) copy-start(bf16[1,192,384]{2,1,0:T(8,128)(2,1)} %copy-done.28) | copy-start | bytes 442372
  199.9 49.7 %copy-start.31 = (bf16[1,192,384]{2,1,0:T(8,128)(2,1)S(1)}, bf16[1,192,384]{2,1,0:T(8,128)(2,1)}, u32[]{:S(2)}) copy-start(bf16[1,192,384]{2,1,0:T(8,128)(2,1)} %copy-done.30) | copy-start | bytes 442372
  199.9 49.7 %copy-start.33 = (bf16[1,192,384]{2,1,0:T(8,128)(2,1)S(1)}, bf16[1,192,384]{2,1,0:T(8,128)(2,1)}, u32[]{:S(2)}) copy-start(bf16[1,192,384]{2,1,0:T(8,128)(2,1)} %copy-done.32) | copy-start | bytes 442372
  199.9 49.7 %copy-start.35 = (bf16[1,192,384]{2,1,0:T(8,128)(2,1)S(1)}, bf16[1,192,384]{2,1,0:T(8,128)(2,1)}, u32[]{:S(2)}) copy-start(bf16[1,192,384]{2,1,0:T(8,128)(2,1)} %copy-done.34) | copy-start | bytes 442372
  (5 other events, 3.5 us)
